TPU v7x, 32 devices: a whole 2x2x4 slice. The times are simulated.
32 devices in a mesh: groups: 2 (over y), expert: 16 (over z, x, core).
Axes of the slice: x: 2, y: 2, z: 4, core: 2. Of those that a mesh axis runs over, the one named last changes fastest.
Arguments:
- tokens: bfloat16 [128, 3072], P(('groups', 'expert')), parts along dimension 0, may hold values from -6 to 6
- cotangent: bfloat16 [128, 3072], P(('groups', 'expert')), parts along dimension 0, may hold values from -6 to 6
- expert_ids: int32 [128, 2], P(('groups', 'expert')), parts along dimension 0, may hold values from 0 to 7, all different within a row; in each aligned block of 4 rows (0 to 3, 4 to 7, ...) at most 2 rows name the same one
- gate_weights: bfloat16 [128, 2], P(('groups', 'expert')), parts along dimension 0, may hold values from 0.19921875 to 1
- w_gate: bfloat16 [65536, 3072], P('expert'), may hold values from -0.109375 to 0.109375
- w_up: bfloat16 [65536, 3072], P('expert'), may hold values from -0.109375 to 0.109375
- w_down: bfloat16 [65536, 3072], P('expert'), may hold values from -0.0625 to 0.0625
Outputs:
- layer_out: bfloat16 [128, 3072], P(('groups', 'expert')), parts along dimension 0
- input_grad: bfloat16 [128, 3072], P(('groups', 'expert')), parts along dimension 0
There are 2 independent parts, one for each index of `groups`. A program takes and returns all parts, laid end to end along the dimension named above; an argument that names none is the same for every part. Nothing has to cross between parts.
Inputs may be any that keep to these rules, and one draw needn't show every extreme that they name: `expert_ids`: each token names two different experts. Among the 8 pairs of one device's tokens no expert is named more than 2 times, a bound that some block reaches.
All inputs are finite; a program needn't handle non-finite values.
Results may differ from a plain program's by a relative error of at most 0.0064.
Values may be sent and summed in bfloat16 or wider, within the bound.
No kernel may reach another device: no remote copies, remote signals or barrier semaphores. Data moves between devices by JAX's collectives and lax.ppermute only.
A program may use at most 192 MiB of HBM per device.

v0:
```python
import jax
import jax.numpy as jnp
from jax import lax
from jax.sharding import PartitionSpec as P

EXPERTS = 8
CAP = 2


def slot_ranks(routes):
    count = routes.shape[-1]
    order = jnp.arange(count, dtype=jnp.int32)
    earlier = order[None, :] < order[:, None]
    same = routes[..., :, None] == routes[..., None, :]
    return jnp.sum(jnp.logical_and(same, earlier), axis=-1)


def owner_work(token_rows, cotan_rows, gate_rows, up_rows, down_rows):
    contract = (((1,), (1,)), ((), ()))
    gate_proj = lax.dot_general(token_rows, gate_rows, contract, preferred_element_type=jnp.float32)
    up_proj = lax.dot_general(token_rows, up_rows, contract, preferred_element_type=jnp.float32)
    sigmoid = jax.nn.sigmoid(gate_proj)
    activated = gate_proj * sigmoid
    hidden = (activated * up_proj).astype(jnp.bfloat16)
    out_part = jnp.dot(hidden, down_rows, preferred_element_type=jnp.float32).astype(jnp.bfloat16)
    hidden_grad = lax.dot_general(
        cotan_rows, down_rows, contract, preferred_element_type=jnp.float32
    )
    gate_grad = (hidden_grad * up_proj * sigmoid * (1.0 + gate_proj * (1.0 - sigmoid))).astype(
        jnp.bfloat16
    )
    up_grad = (hidden_grad * activated).astype(jnp.bfloat16)
    grad_part = jnp.dot(gate_grad, gate_rows, preferred_element_type=jnp.float32)
    grad_part = grad_part + jnp.dot(up_grad, up_rows, preferred_element_type=jnp.float32)
    return (out_part, grad_part.astype(jnp.bfloat16))


def shards(tokens, cotangent, expert_ids, gate_weights, w_gate, w_up, w_down):
    devices = lax.axis_size("expert")
    owner_count = devices // EXPERTS
    tok_count = tokens.shape[0]
    features = tokens.shape[1]
    pair_count = tok_count * 2
    routes = expert_ids.reshape(pair_count)
    rank_index = slot_ranks(routes)
    slot_index = routes * CAP + rank_index
    token_pairs = jnp.repeat(tokens, 2, axis=0)
    scaled = (
        gate_weights.reshape(pair_count, 1).astype(jnp.float32)
        * jnp.repeat(cotangent, 2, axis=0).astype(jnp.float32)
    ).astype(jnp.bfloat16)
    token_slots = jnp.zeros((EXPERTS * CAP, features), jnp.bfloat16).at[slot_index].set(token_pairs)
    cotan_slots = jnp.zeros((EXPERTS * CAP, features), jnp.bfloat16).at[slot_index].set(scaled)
    send_tokens = jnp.repeat(token_slots.reshape(EXPERTS, CAP, features), owner_count, axis=0)
    send_cotan = jnp.repeat(cotan_slots.reshape(EXPERTS, CAP, features), owner_count, axis=0)
    token_rows = lax.all_to_all(send_tokens, "expert", split_axis=0, concat_axis=0, tiled=True)
    cotan_rows = lax.all_to_all(send_cotan, "expert", split_axis=0, concat_axis=0, tiled=True)
    shape = token_rows.shape
    out_part, grad_part = owner_work(
        token_rows.reshape(-1, features), cotan_rows.reshape(-1, features), w_gate, w_up, w_down
    )
    out_part, grad_part = (out_part.reshape(shape), grad_part.reshape(shape))
    home_out, home_grad = (
        lax.all_to_all(out_part, "expert", split_axis=0, concat_axis=0, tiled=True),
        lax.all_to_all(grad_part, "expert", split_axis=0, concat_axis=0, tiled=True),
    )
    out_sum = jnp.sum(
        home_out.reshape(EXPERTS, owner_count, CAP, features).astype(jnp.float32), axis=1
    ).reshape(EXPERTS * CAP, features)
    grad_sum = jnp.sum(
        home_grad.reshape(EXPERTS, owner_count, CAP, features).astype(jnp.float32), axis=1
    ).reshape(EXPERTS * CAP, features)
    picked_out = out_sum[slot_index].reshape(tok_count, 2, features)
    picked_grad = grad_sum[slot_index].reshape(tok_count, 2, features)
    layer_out = jnp.sum(picked_out * gate_weights.astype(jnp.float32)[:, :, None], axis=1).astype(
        jnp.bfloat16
    )
    input_grad = jnp.sum(picked_grad, axis=1).astype(jnp.bfloat16)
    return (layer_out, input_grad)


def solution(mesh):
    in_specs = (
        P(("groups", "expert"), None),
        P(("groups", "expert"), None),
        P(("groups", "expert"), None),
        P(("groups", "expert"), None),
        P("expert", None),
        P("expert", None),
        P("expert", None),
    )
    out_specs = (P(("groups", "expert"), None), P(("groups", "expert"), None))
    return jax.shard_map(shards, mesh=mesh, in_specs=in_specs, out_specs=out_specs, check_vma=False)
```

profile of v0, /device:TPU:0, one launch (start us, length us, event | category | flops | bytes accessed | tf_op | source)
XLA Modules:
  0.0 117.9 jit_solution(2926665202250417678)
XLA Ops:
  0.6 0.7 broadcast_multiply_fusion
  1.3 0.8 copy.18
  2.1 0.1 copy.17
  2.2 0.1 mul.51
  2.3 0.1 eq.15
  2.3 0.2 convert_reduce_fusion.2
  2.5 0.8 broadcast_in_dim.8
  3.3 0.7 scatter_custom_fusion
  4.1 0.8 broadcast_in_dim.9
  4.9 7.4 %all-to-all-start = ((bf16[16,2,3072]{2,1,0:T(2,128)(2,1)}), bf16[16,2,3072]{2,1,0:T(2,128)(2,1)S(1)}, u32[]{:S(2)}, u32[]{:S(2)}) async-start(bf16[16,2,3072]{2,1,0:T(2,128)(2,1)} %bitcast.2), calls=%async_computation | async-start | bytes 393216 | tf_op jit(solution)/shard_map/all_to_all | solution.py:56
  12.3 0.8 copy.19
  13.0 0.8 broadcast_in_dim.10
  13.8 0.1 convert_element_type.70
  13.9 0.1 reshape.107
  13.9 0.8 scatter_custom_fusion.1
  14.8 6.5 %all-to-all-done = bf16[16,2,3072]{2,1,0:T(2,128)(2,1)S(1)} async-done(((bf16[16,2,3072]{2,1,0:T(2,128)(2,1)}), bf16[16,2,3072]{2,1,0:T(2,128)(2,1)S(1)}, u32[]{:S(2)}, u32[]{:S(2)}) %all-to-all-start) | async-done | bytes 196640 | tf_op jit(solution)/shard_map/all_to_all | solution.py:56
  21.2 0.8 broadcast_in_dim.22
  22.0 3.5 %all-to-all-start.2 = ((bf16[16,2,3072]{2,1,0:T(2,128)(2,1)}), bf16[16,2,3072]{2,1,0:T(2,128)(2,1)S(1)}, u32[]{:S(2)}, u32[]{:S(2)}) async-start(bf16[16,2,3072]{2,1,0:T(2,128)(2,1)} %bitcast.4), calls=%async_computation.2 | async-start | bytes 393216 | tf_op jit(solution)/shard_map/all_to_all | solution.py:57
  25.5 0.1 reshape.96
  25.6 12.2 %fusion.17 = f32[32,4096]{1,0:T(8,128)S(1)} fusion(bf16[32,3072]{1,0:T(8,128)(2,1)S(1)} %reshape.96, bf16[4096,3072]{1,0:T(8,128)(2,1)} %param.12), kind=kOutput, calls=%fused_computation.35 | convolution fusion | flops 805306368 | bytes 25886720 | tf_op jit(solution)/shard_map/dot_general | solution.py:21
  37.8 12.2 %fusion.16 = f32[32,4096]{1,0:T(8,128)S(1)} fusion(bf16[32,3072]{1,0:T(8,128)(2,1)S(1)} %reshape.96, bf16[4096,3072]{1,0:T(8,128)(2,1)} %param.11), kind=kOutput, calls=%fused_computation.34 | convolution fusion | flops 805306368 | bytes 25886720 | tf_op jit(solution)/shard_map/dot_general | solution.py:20
  50.0 10.5 %convolution_convert_fusion = bf16[32,3072]{1,0:T(8,128)(2,1)S(1)} fusion(bf16[4096,3072]{1,0:T(8,128)(2,1)} %param.13, f32[32,4096]{1,0:T(8,128)S(1)} %fusion.17, f32[32,4096]{1,0:T(8,128)S(1)} %fusion.16), kind=kOutput, calls=%fused_computation.6 | convolution fusion | flops 806191104 | bytes 26411008 | tf_op jit(solution)/shard_map/dot_general | solution.py:25
  60.5 0.7 reshape.97
  61.2 0.0 all-to-all-done.2
  61.2 6.0 %all-to-all-start.1 = ((bf16[16,2,3072]{2,1,0:T(2,128)(2,1)}), bf16[16,2,3072]{2,1,0:T(2,128)(2,1)S(1)}, u32[]{:S(2)}, u32[]{:S(2)}) async-start(bf16[16,2,3072]{2,1,0:T(2,128)(2,1)} %reshape.97), calls=%async_computation.1 | async-start | bytes 393216 | tf_op jit(solution)/shard_map/all_to_all | solution.py:64
  67.2 0.1 reshape.102
  67.3 12.2 %fusion.18 = f32[32,4096]{1,0:T(8,128)S(1)} fusion(bf16[32,3072]{1,0:T(8,128)(2,1)S(1)} %reshape.102, bf16[4096,3072]{1,0:T(8,128)(2,1)} %param.13), kind=kOutput, calls=%fused_computation.36 | convolution fusion | flops 805306368 | bytes 25886720 | tf_op jit(solution)/shard_map/dot_general | solution.py:26
  79.5 10.4 %fusion.2 = f32[32,3072]{1,0:T(8,128)S(1)} fusion(bf16[4096,3072]{1,0:T(8,128)(2,1)} %param.11, f32[32,4096]{1,0:T(8,128)S(1)} %fusion.16, f32[32,4096]{1,0:T(8,128)S(1)} %fusion.18, f32[32,4096]{1,0:T(8,128)S(1)} %fusion.17), kind=kOutput, calls=%fused_computation.14 | convolution fusion | flops 806617088 | bytes 27131904 | tf_op jit(solution)/shard_map/dot_general | solution.py:33
  89.9 10.5 %fusion = bf16[32,3072]{1,0:T(8,128)(2,1)S(1)} fusion(f32[32,3072]{1,0:T(8,128)S(1)} %fusion.2, bf16[4096,3072]{1,0:T(8,128)(2,1)} %param.12, f32[32,4096]{1,0:T(8,128)S(1)} %fusion.18, f32[32,4096]{1,0:T(8,128)S(1)} %fusion.16), kind=kOutput, calls=%fused_computation.5 | convolution fusion | flops 806289408 | bytes 26804224 | tf_op jit(solution)/shard_map/dot_general | solution.py:34
  100.4 0.8 reshape.103
  101.2 0.0 all-to-all-done.1
  101.2 6.0 %all-to-all-start.3 = ((bf16[16,2,3072]{2,1,0:T(2,128)(2,1)}), bf16[16,2,3072]{2,1,0:T(2,128)(2,1)S(1)}, u32[]{:S(2)}, u32[]{:S(2)}) async-start(bf16[16,2,3072]{2,1,0:T(2,128)(2,1)} %reshape.103), calls=%async_computation.3 | async-start | bytes 393216 | tf_op jit(solution)/shard_map/all_to_all | solution.py:65
  107.2 0.2 convert_reduce_fusion.1
  107.4 0.1 reshape.98
  107.6 0.6 gather_fusion
  108.2 0.1 reshape.99
  108.2 0.8 multiply_reduce_fusion
  109.0 7.1 %all-to-all-done.3 = bf16[16,2,3072]{2,1,0:T(2,128)(2,1)S(1)} async-done(((bf16[16,2,3072]{2,1,0:T(2,128)(2,1)}), bf16[16,2,3072]{2,1,0:T(2,128)(2,1)S(1)}, u32[]{:S(2)}, u32[]{:S(2)}) %all-to-all-start.3) | async-done | bytes 196640 | tf_op jit(solution)/shard_map/all_to_all | solution.py:65
  116.2 0.2 convert_reduce_fusion
  116.4 0.1 reshape.104
  116.5 0.6 gather_fusion.1
  117.1 0.1 reshape.105
  117.2 0.7 reduce_sum.52
  (5 shorter events, 0.1 us)
Async XLA Ops:
  4.9 16.4 %all-to-all-start = ((bf16[16,2,3072]{2,1,0:T(2,128)(2,1)}), bf16[16,2,3072]{2,1,0:T(2,128)(2,1)S(1)}, u32[]{:S(2)}, u32[]{:S(2)}) async-start(bf16[16,2,3072]{2,1,0:T(2,128)(2,1)} %bitcast.2), calls=%async_computation | async-start | bytes 393216 | tf_op jit(solution)/shard_map/all_to_all | solution.py:56
  22.0 39.2 %all-to-all-start.2 = ((bf16[16,2,3072]{2,1,0:T(2,128)(2,1)}), bf16[16,2,3072]{2,1,0:T(2,128)(2,1)S(1)}, u32[]{:S(2)}, u32[]{:S(2)}) async-start(bf16[16,2,3072]{2,1,0:T(2,128)(2,1)} %bitcast.4), calls=%async_computation.2 | async-start | bytes 393216 | tf_op jit(solution)/shard_map/all_to_all | solution.py:57
  61.2 40.0 %all-to-all-start.1 = ((bf16[16,2,3072]{2,1,0:T(2,128)(2,1)}), bf16[16,2,3072]{2,1,0:T(2,128)(2,1)S(1)}, u32[]{:S(2)}, u32[]{:S(2)}) async-start(bf16[16,2,3072]{2,1,0:T(2,128)(2,1)} %reshape.97), calls=%async_computation.1 | async-start | bytes 393216 | tf_op jit(solution)/shard_map/all_to_all | solution.py:64
  101.2 15.0 %all-to-all-start.3 = ((bf16[16,2,3072]{2,1,0:T(2,128)(2,1)}), bf16[16,2,3072]{2,1,0:T(2,128)(2,1)S(1)}, u32[]{:S(2)}, u32[]{:S(2)}) async-start(bf16[16,2,3072]{2,1,0:T(2,128)(2,1)} %reshape.103), calls=%async_computation.3 | async-start | bytes 393216 | tf_op jit(solution)/shard_map/all_to_all | solution.py:65
where the time goes:
time: 119 us; the launch traced here: 118 us
  matrix products  68 us (57%)
  starting transfers between devices  22.9 us (19%)
  waiting for transfers between devices  13.6 us (11%)
  local copies, waits for them, and re-layouts  9.06 us (8%)
  other arithmetic  3.62 us (3%)
    dot_general x1, matrix products, owner_work(): lax.dot_general(token_rows, gate_rows, contract, preferred_element_type=j...  12.2 us
    dot_general x1, matrix products, owner_work(): lax.dot_general(cotan_rows, down_rows, contract, preferred_element_type=j...  12.2 us
    dot_general x1, matrix products, owner_work(): lax.dot_general(token_rows, up_rows, contract, preferred_element_type=jnp...  12.2 us
    dot_general x1, matrix products, owner_work(): jnp.dot(up_grad, up_rows, preferred_element_type=jnp.float32)  10.5 us
    dot_general x1, matrix products, owner_work(): jnp.dot(hidden, down_rows, preferred_element_type=jnp.float32)  10.5 us
    dot_general x1, matrix products, owner_work(): jnp.dot(gate_grad, gate_rows, preferred_element_type=jnp.float32)  10.4 us
    all_to_all x1, starting transfers between devices, shards(): lax.all_to_all(send_tokens, 'expert', split_axis=0, concat_axis=0, tiled=...  7.39 us
    all_to_all x1, waiting for transfers between devices, shards(): lax.all_to_all(grad_part, 'expert', split_axis=0, concat_axis=0, tiled=True)  7.11 us
  transfers between devices with their start and end apart: 4, of which 2 were waited for; matrix products, arithmetic and copies ran while one was open for 63% of the time, Pallas kernels for 0%

commit v1 on v0

v1 whole, which is shorter than its diff:
```python
import functools

import jax
import jax.numpy as jnp
from jax import lax
from jax.experimental import pallas as pl
from jax.experimental.pallas import tpu as pltpu
from jax.sharding import PartitionSpec as P

EXPERTS = 8
CAP = 2
NT = (((1,), (1,)), ((), ()))


def slot_ranks(routes):
    count = routes.shape[-1]
    order = jnp.arange(count, dtype=jnp.int32)
    earlier = order[None, :] < order[:, None]
    same = routes[..., :, None] == routes[..., None, :]
    return jnp.sum(jnp.logical_and(same, earlier), axis=-1)


def expert_kernel(x_ref, c_ref, wg_ref, wu_ref, wd_ref, out_ref, grad_ref, acc_out, acc_grad):
    step = pl.program_id(0)

    @pl.when(step == 0)
    def _():
        acc_out[...] = jnp.zeros_like(acc_out)
        acc_grad[...] = jnp.zeros_like(acc_grad)

    x = x_ref[...]
    c = c_ref[...]
    wg = wg_ref[...]
    wu = wu_ref[...]
    wd = wd_ref[...]
    gate_proj = lax.dot_general(x, wg, NT, preferred_element_type=jnp.float32)
    up_proj = lax.dot_general(x, wu, NT, preferred_element_type=jnp.float32)
    sigmoid = jax.nn.sigmoid(gate_proj)
    activated = gate_proj * sigmoid
    hidden = (activated * up_proj).astype(jnp.bfloat16)
    acc_out[...] += jnp.dot(hidden, wd, preferred_element_type=jnp.float32)
    hidden_grad = lax.dot_general(c, wd, NT, preferred_element_type=jnp.float32)
    gate_grad = (hidden_grad * up_proj * sigmoid * (1.0 + gate_proj * (1.0 - sigmoid))).astype(
        jnp.bfloat16
    )
    up_grad = (hidden_grad * activated).astype(jnp.bfloat16)
    acc_grad[...] += jnp.dot(gate_grad, wg, preferred_element_type=jnp.float32) + jnp.dot(
        up_grad, wu, preferred_element_type=jnp.float32
    )

    @pl.when(step == pl.num_programs(0) - 1)
    def _():
        out_ref[...] = acc_out[...].astype(out_ref.dtype)
        grad_ref[...] = acc_grad[...].astype(grad_ref.dtype)


def expert_work(rows, w_gate, w_up, w_down):
    m = rows.shape[0]
    hidden_units, features = w_gate.shape
    block = min(512, hidden_units)
    steps = hidden_units // block
    row_spec = lambda half: pl.BlockSpec((m, features), lambda i: (0, half))
    w_spec = pl.BlockSpec((block, features), lambda i: (i, 0))
    out_spec = pl.BlockSpec((m, features), lambda i: (0, 0))
    cost = pl.CostEstimate(
        flops=12 * m * hidden_units * features,
        transcendentals=m * hidden_units,
        bytes_accessed=3 * hidden_units * features * 2 + 4 * m * features * 2,
    )
    return pl.pallas_call(
        expert_kernel,
        grid=(steps,),
        in_specs=[row_spec(0), row_spec(1), w_spec, w_spec, w_spec],
        out_specs=[out_spec, out_spec],
        out_shape=[jax.ShapeDtypeStruct((m, features), jnp.bfloat16)] * 2,
        scratch_shapes=[pltpu.VMEM((m, features), jnp.float32)] * 2,
        compiler_params=pltpu.CompilerParams(
            dimension_semantics=("arbitrary",), vmem_limit_bytes=48 * 1024 * 1024
        ),
        cost_estimate=cost,
    )(rows, rows, w_gate, w_up, w_down)


def shards(tokens, cotangent, expert_ids, gate_weights, w_gate, w_up, w_down):
    devices = lax.axis_size("expert")
    owner_count = devices // EXPERTS
    tok_count = tokens.shape[0]
    features = tokens.shape[1]
    pair_count = tok_count * 2
    routes = expert_ids.reshape(pair_count)
    rank_index = slot_ranks(routes)
    slot_index = routes * CAP + rank_index
    token_pairs = jnp.repeat(tokens, 2, axis=0)
    scaled = (
        gate_weights.reshape(pair_count, 1).astype(jnp.float32)
        * jnp.repeat(cotangent, 2, axis=0).astype(jnp.float32)
    ).astype(jnp.bfloat16)
    both = jnp.concatenate([token_pairs, scaled], axis=1)
    slots = jnp.zeros((EXPERTS * CAP, 2 * features), jnp.bfloat16).at[slot_index].set(both)
    send = jnp.repeat(slots.reshape(EXPERTS, CAP, 2 * features), owner_count, axis=0)
    recv = lax.all_to_all(send, "expert", split_axis=0, concat_axis=0, tiled=True)
    shape = (devices, CAP, features)
    out_part, grad_part = expert_work(recv.reshape(-1, 2 * features), w_gate, w_up, w_down)
    back = jnp.concatenate([out_part.reshape(shape), grad_part.reshape(shape)], axis=2)
    home = lax.all_to_all(back, "expert", split_axis=0, concat_axis=0, tiled=True)
    sums = jnp.sum(
        home.reshape(EXPERTS, owner_count, CAP, 2 * features).astype(jnp.float32), axis=1
    ).reshape(EXPERTS * CAP, 2 * features)
    picked = sums[slot_index].reshape(tok_count, 2, 2 * features)
    picked_out = picked[:, :, :features]
    picked_grad = picked[:, :, features:]
    layer_out = jnp.sum(picked_out * gate_weights.astype(jnp.float32)[:, :, None], axis=1).astype(
        jnp.bfloat16
    )
    input_grad = jnp.sum(picked_grad, axis=1).astype(jnp.bfloat16)
    return (layer_out, input_grad)


def solution(mesh):
    in_specs = (
        P(("groups", "expert"), None),
        P(("groups", "expert"), None),
        P(("groups", "expert"), None),
        P(("groups", "expert"), None),
        P("expert", None),
        P("expert", None),
        P("expert", None),
    )
    out_specs = (P(("groups", "expert"), None), P(("groups", "expert"), None))
    return jax.shard_map(shards, mesh=mesh, in_specs=in_specs, out_specs=out_specs, check_vma=False)
```

time: 119 us -> 86.6 us (0.73)
  matrix products: 68 us -> 0 us
  Pallas kernels: 0 us -> 41.1 us
  blocking collectives: 0 us -> 19.4 us
  starting transfers between devices: 22.9 us -> 3.55 us
  local copies, waits for them, and re-layouts: 9.06 us -> 5.15 us
  waiting for transfers between devices: 13.6 us -> 12.1 us
    dot_general x6 -> x0, matrix products: 68 us -> none  [the longest x1 12.2 us: owner_work(): lax.dot_general(token_rows, gate_rows, contract, preferred_element_type=j...]
    pallas_call x0 -> x1, Pallas kernels: none -> 41.1 us  [expert_work(): pl.pallas_call(expert_kernel, grid=(steps,), in_specs=[row_spec(0), row_s...]
    all_to_all x0 -> x1, blocking collectives: none -> 19.4 us  [shards(): lax.all_to_all(send, 'expert', split_axis=0, concat_axis=0, tiled=True)]
    all_to_all x4 -> x1, starting transfers between devices: 22.9 us -> 3.55 us  [shards(): lax.all_to_all(back, 'expert', split_axis=0, concat_axis=0, tiled=True)]
    all_to_all x4 -> x1, waiting for transfers between devices: 13.6 us -> 12.1 us  [shards(): lax.all_to_all(back, 'expert', split_axis=0, concat_axis=0, tiled=True)]
    broadcast_in_dim x2 -> x1, local copies, waits for them, and re-layouts: 1.56 us -> 0.21 us  [shards(): jnp.repeat(slots.reshape(EXPERTS, CAP, 2 * features), owner_count, axis=0)]
    reshape x10 -> x6, local copies, waits for them, and re-layouts: 2.13 us -> 0.84 us  [the longest x1 0.27 us: shards(): sums = jnp.sum(home.reshape(EXPERTS, owner_count, CAP, 2 * features).asty...]
  transfers between devices with their start and end apart: 4 -> 1, of which waited for: 2 -> 1; matrix products, arithmetic and copies ran while one was open for 63% -> 0% of each run, Pallas kernels for 0% -> 0%
where the time goes in v1:
time: 86.6 us; the launch traced here: 86.2 us
  Pallas kernels  41.1 us (47%)
  blocking collectives  19.4 us (22%)
  waiting for transfers between devices  12.1 us (14%)
  local copies, waits for them, and re-layouts  5.15 us (6%)
  other arithmetic  4.17 us (5%)
  starting transfers between devices  3.55 us (4%)
    pallas_call x1, Pallas kernels, expert_work(): pl.pallas_call(expert_kernel, grid=(steps,), in_specs=[row_spec(0), row_s...  41.1 us
    all_to_all x1, blocking collectives, shards(): lax.all_to_all(send, 'expert', split_axis=0, concat_axis=0, tiled=True)  19.4 us
    all_to_all x1, waiting for transfers between devices, shards(): lax.all_to_all(back, 'expert', split_axis=0, concat_axis=0, tiled=True)  12.1 us
    all_to_all x1, starting transfers between devices, shards(): lax.all_to_all(back, 'expert', split_axis=0, concat_axis=0, tiled=True)  3.55 us
  transfers between devices with their start and end apart: 1, of which 1 were waited for; matrix products, arithmetic and copies ran while one was open for 0% of the time, Pallas kernels for 0%

profile of v1, /device:TPU:0, one launch (start us, length us, event | category | flops | bytes accessed | tf_op | source)
XLA Modules:
  0.0 86.2 jit_solution(11443547153744800219)
XLA Ops:
  0.6 0.7 broadcast_multiply_fusion
  1.3 0.8 copy.18
  2.1 0.7 copy.19
  2.8 0.1 reshape.83
  2.9 0.8 broadcast_in_dim.19
  3.7 0.1 convert_element_type.43
  3.8 0.1 copy.17
  3.9 0.1 mul.30
  3.9 0.1 eq.15
  4.0 0.2 convert_reduce_fusion.1
  4.2 0.8 broadcast_in_dim.18
  5.0 0.1 multiply_convert_fusion
  5.1 0.8 scatter_custom_fusion
  5.9 0.1 reshape.76
  6.1 0.2 broadcast_in_dim.20
  6.3 19.4 %all_to_all.10 = bf16[16,2,6144]{2,1,0:T(2,128)(2,1)S(1)} all-to-all(bf16[16,2,6144]{2,1,0:T(2,128)(2,1)S(1)} %bitcast.10), channel_id=1, replica_groups=mesh['groups'=2,'expert'=16] {'expert'}, dimensions={0} | all-to-all | bytes 786432 | tf_op jit(solution)/shard_map/all_to_all | solution.py:101
  25.6 0.1 reshape.78.x_ref.c_ref
  25.8 41.1 %shard_map.86 = (bf16[32,3072]{1,0:T(8,128)(2,1)S(1)}, bf16[32,3072]{1,0:T(8,128)(2,1)S(1)}) custom-call(bf16[32,6144]{1,0:T(8,128)(2,1)S(1)} %reshape.78.x_ref.c_ref, bf16[32,6144]{1,0:T(8,128)(2,1)S(1)} %reshape.78.x_ref.c_ref, bf16[4096,3072]{1,0:T(8,128)(2,1)} %wg_ref.1, bf16[4096,3072]{1,0:T(8,128)(2,1)} %wu_ref.1, bf16[4096,3072]{1,0:T(8,128)(2,1)} %wd_ref.1), custom_call_target="tpu_custom_call" | custom-call | flops 4831838208 | bytes 76283904 | tf_op jit(solution)/shard_map/pallas_call | solution.py:70
  66.9 0.1 reshape.79
  67.0 0.1 reshape.80
  67.1 1.1 %pad_maximum_fusion = bf16[16,2,6144]{2,1,0:T(2,128)(2,1)} fusion(bf16[16,2,3072]{2,1,0:T(2,128)(2,1)S(1)} %reshape.80, bf16[16,2,3072]{2,1,0:T(2,128)(2,1)S(1)} %reshape.79), kind=kLoop, calls=%fused_computation.3 | loop fusion | flops 786432 | bytes 786432 | tf_op jit(solution)/shard_map/concatenate | solution.py:104
  68.2 3.6 %all-to-all-start.1 = ((bf16[16,2,6144]{2,1,0:T(2,128)(2,1)}), bf16[16,2,6144]{2,1,0:T(2,128)(2,1)S(1)}, u32[]{:S(2)}, u32[]{:S(2)}) async-start(bf16[16,2,6144]{2,1,0:T(2,128)(2,1)} %pad_maximum_fusion), calls=%async_computation.1 | async-start | bytes 786432 | tf_op jit(solution)/shard_map/all_to_all | solution.py:105
  71.7 12.1 %all-to-all-done.1 = bf16[16,2,6144]{2,1,0:T(2,128)(2,1)S(1)} async-done(((bf16[16,2,6144]{2,1,0:T(2,128)(2,1)}), bf16[16,2,6144]{2,1,0:T(2,128)(2,1)S(1)}, u32[]{:S(2)}, u32[]{:S(2)}) %all-to-all-start.1) | async-done | bytes 393248 | tf_op jit(solution)/shard_map/all_to_all | solution.py:105
  83.9 0.4 convert_reduce_fusion
  84.3 0.3 reshape.81
  84.6 0.6 gather_fusion
  85.2 0.1 reshape.82
  85.3 0.9 %slice_reduce_fusion = (bf16[4,3072]{1,0:T(4,128)(2,1)}, bf16[4,3072]{1,0:T(4,128)(2,1)}) fusion(f32[4,2,6144]{2,1,0:T(2,128)S(1)} %reshape.82, f32[4,2]{1,0:T(4,128)S(1)} %copy.19), kind=kLoop, calls=%fused_computation.4 | loop fusion | flops 49152 | bytes 245792 | tf_op jit(solution)/shard_map/reduce_sum | solution.py:115
  (3 shorter events, 0.0 us)
Async XLA Ops:
  68.2 15.7 %all-to-all-start.1 = ((bf16[16,2,6144]{2,1,0:T(2,128)(2,1)}), bf16[16,2,6144]{2,1,0:T(2,128)(2,1)S(1)}, u32[]{:S(2)}, u32[]{:S(2)}) async-start(bf16[16,2,6144]{2,1,0:T(2,128)(2,1)} %pad_maximum_fusion), calls=%async_computation.1 | async-start | bytes 786432 | tf_op jit(solution)/shard_map/all_to_all | solution.py:105

commit v2 on v1

--- a/solution.py
+++ b/solution.py
@@ -20,8 +20,9 @@
     return jnp.sum(jnp.logical_and(same, earlier), axis=-1)
 
 
-def expert_kernel(x_ref, c_ref, wg_ref, wu_ref, wd_ref, out_ref, grad_ref, acc_out, acc_grad):
+def expert_kernel(offset_ref, x_ref, c_ref, wg_ref, wu_ref, wd_ref, out_ref, acc_out, acc_grad):
     step = pl.program_id(0)
+    features = acc_out.shape[1]
 
     @pl.when(step == 0)
     def _():
@@ -50,39 +51,47 @@
 
     @pl.when(step == pl.num_programs(0) - 1)
     def _():
-        out_ref[...] = acc_out[...].astype(out_ref.dtype)
-        grad_ref[...] = acc_grad[...].astype(grad_ref.dtype)
+        out_ref[:, :features] = acc_out[...].astype(out_ref.dtype)
+        out_ref[:, features:] = acc_grad[...].astype(out_ref.dtype)
 
 
-def expert_work(rows, w_gate, w_up, w_down):
+def expert_work(rows, w_gate, w_up, w_down, part, parts):
     m = rows.shape[0]
     hidden_units, features = w_gate.shape
-    block = min(512, hidden_units)
-    steps = hidden_units // block
-    row_spec = lambda half: pl.BlockSpec((m, features), lambda i: (0, half))
-    w_spec = pl.BlockSpec((block, features), lambda i: (i, 0))
-    out_spec = pl.BlockSpec((m, features), lambda i: (0, 0))
+    share = hidden_units // parts
+    block = min(256, share)
+    steps = share // block
+    offset = jnp.reshape(part * steps, (1,)).astype(jnp.int32)
+    row_spec = lambda half: pl.BlockSpec((m, features), lambda i, off: (0, half))
+    w_spec = pl.BlockSpec((block, features), lambda i, off: (off[0] + i, 0))
+    out_spec = pl.BlockSpec((m, 2 * features), lambda i, off: (0, 0))
     cost = pl.CostEstimate(
-        flops=12 * m * hidden_units * features,
-        transcendentals=m * hidden_units,
-        bytes_accessed=3 * hidden_units * features * 2 + 4 * m * features * 2,
+        flops=12 * m * share * features,
+        transcendentals=m * share,
+        bytes_accessed=3 * share * features * 2 + 4 * m * features * 2,
+    )
+    grid_spec = pltpu.PrefetchScalarGridSpec(
+        num_scalar_prefetch=1,
+        grid=(steps,),
+        in_specs=[row_spec(0), row_spec(1), w_spec, w_spec, w_spec],
+        out_specs=out_spec,
+        scratch_shapes=[pltpu.VMEM((m, features), jnp.float32)] * 2,
     )
     return pl.pallas_call(
         expert_kernel,
-        grid=(steps,),
-        in_specs=[row_spec(0), row_spec(1), w_spec, w_spec, w_spec],
-        out_specs=[out_spec, out_spec],
-        out_shape=[jax.ShapeDtypeStruct((m, features), jnp.bfloat16)] * 2,
-        scratch_shapes=[pltpu.VMEM((m, features), jnp.float32)] * 2,
+        grid_spec=grid_spec,
+        out_shape=jax.ShapeDtypeStruct((m, 2 * features), jnp.bfloat16),
         compiler_params=pltpu.CompilerParams(
             dimension_semantics=("arbitrary",), vmem_limit_bytes=48 * 1024 * 1024
         ),
         cost_estimate=cost,
-    )(rows, rows, w_gate, w_up, w_down)
+    )(offset, rows, rows, w_gate, w_up, w_down)
 
 
 def shards(tokens, cotangent, expert_ids, gate_weights, w_gate, w_up, w_down):
     devices = lax.axis_size("expert")
+    parts = lax.axis_size("groups")
+    part = lax.axis_index("groups")
     owner_count = devices // EXPERTS
     tok_count = tokens.shape[0]
     features = tokens.shape[1]
@@ -98,13 +107,15 @@
     both = jnp.concatenate([token_pairs, scaled], axis=1)
     slots = jnp.zeros((EXPERTS * CAP, 2 * features), jnp.bfloat16).at[slot_index].set(both)
     send = jnp.repeat(slots.reshape(EXPERTS, CAP, 2 * features), owner_count, axis=0)
-    recv = lax.all_to_all(send, "expert", split_axis=0, concat_axis=0, tiled=True)
-    shape = (devices, CAP, features)
-    out_part, grad_part = expert_work(recv.reshape(-1, 2 * features), w_gate, w_up, w_down)
-    back = jnp.concatenate([out_part.reshape(shape), grad_part.reshape(shape)], axis=2)
-    home = lax.all_to_all(back, "expert", split_axis=0, concat_axis=0, tiled=True)
+    send = jnp.tile(send, (parts, 1, 1))
+    axes = ("groups", "expert")
+    recv = lax.all_to_all(send, axes, split_axis=0, concat_axis=0, tiled=True)
+    partials = expert_work(recv.reshape(-1, 2 * features), w_gate, w_up, w_down, part, parts)
+    back = partials.reshape(parts * devices, CAP, 2 * features)
+    home = lax.all_to_all(back, axes, split_axis=0, concat_axis=0, tiled=True)
     sums = jnp.sum(
-        home.reshape(EXPERTS, owner_count, CAP, 2 * features).astype(jnp.float32), axis=1
+        home.reshape(parts, EXPERTS, owner_count, CAP, 2 * features).astype(jnp.float32),
+        axis=(0, 2),
     ).reshape(EXPERTS * CAP, 2 * features)
     picked = sums[slot_index].reshape(tok_count, 2, 2 * features)
     picked_out = picked[:, :, :features]

time: 86.6 us -> 94.2 us (1.088)
  waiting for transfers between devices: 12.1 us -> 43 us
  blocking collectives: 19.4 us -> 0 us
  Pallas kernels: 41.1 us -> 28.9 us
  starting transfers between devices: 3.55 us -> 9.95 us
  local copies, waits for them, and re-layouts: 5.15 us -> 7.81 us
    all_to_all x1 -> x2, waiting for transfers between devices: 12.1 us -> 43 us  [the longest x1 21.5 us: shards(): recv = lax.all_to_all(send, axes, split_axis=0, concat_axis=0, tiled=True)]
    all_to_all x1 -> x0, blocking collectives: 19.4 us -> none  [shards(): lax.all_to_all(send, 'expert', split_axis=0, concat_axis=0, tiled=True)]
    pallas_call x1, Pallas kernels: 41.1 us -> 28.9 us  [expert_work(): pl.pallas_call(expert_kernel, grid_spec=grid_spec, out_shape=jax.ShapeDty...]
    all_to_all x1 -> x2, starting transfers between devices: 3.55 us -> 9.95 us  [the longest x1 7.33 us: shards(): recv = lax.all_to_all(send, axes, split_axis=0, concat_axis=0, tiled=True)]
    another operation x0 -> x1, local copies, waits for them, and re-layouts: none -> 1.29 us  [shards(): send = jnp.tile(send, (parts, 1, 1))]
    reshape x3 -> x2, local copies, waits for them, and re-layouts: 0.42 us -> 1.65 us  [the longest x1 1.38 us: shards(): back = partials.reshape(parts * devices, CAP, 2 * features)]
    concatenate x1 -> x0, other arithmetic: 1.09 us -> none  [shards(): jnp.concatenate([out_part.reshape(shape), grad_part.reshape(shape)], axis=2)]
  transfers between devices with their start and end apart: 1 -> 2, of which waited for: 1 -> 2; matrix products, arithmetic and copies ran while one was open for 0% -> 0% of each run, Pallas kernels for 0% -> 0%
where the time goes in v2:
time: 94.2 us; the launch traced here: 93.8 us
  waiting for transfers between devices  43 us (46%)
  Pallas kernels  28.9 us (31%)
  starting transfers between devices  9.95 us (11%)
  local copies, waits for them, and re-layouts  7.81 us (8%)
  other arithmetic  3.38 us (4%)
    pallas_call x1, Pallas kernels, expert_work(): pl.pallas_call(expert_kernel, grid_spec=grid_spec, out_shape=jax.ShapeDty...  28.9 us
    all_to_all x1, waiting for transfers between devices, shards(): recv = lax.all_to_all(send, axes, split_axis=0, concat_axis=0, tiled=True)  21.5 us
    all_to_all x1, waiting for transfers between devices, shards(): home = lax.all_to_all(back, axes, split_axis=0, concat_axis=0, tiled=True)  21.5 us
    all_to_all x1, starting transfers between devices, shards(): recv = lax.all_to_all(send, axes, split_axis=0, concat_axis=0, tiled=True)  7.33 us
    all_to_all x1, starting transfers between devices, shards(): home = lax.all_to_all(back, axes, split_axis=0, concat_axis=0, tiled=True)  2.62 us
  transfers between devices with their start and end apart: 2, of which 2 were waited for; matrix products, arithmetic and copies ran while one was open for 0% of the time, Pallas kernels for 0%

profile of v2, /device:TPU:0, one launch (start us, length us, event | category | flops | bytes accessed | tf_op | source)
XLA Modules:
  0.0 93.8 jit_solution(10771240065258274302)
XLA Ops:
  0.6 0.7 broadcast_multiply_fusion
  1.3 0.8 copy.18
  2.1 0.7 copy.19
  2.8 0.1 reshape.83
  2.9 0.8 broadcast_in_dim.19
  3.7 0.1 convert_element_type.43
  3.8 0.1 copy.17
  3.9 0.1 mul.34
  3.9 0.1 eq.15
  4.0 0.2 convert_reduce_fusion.1
  4.2 0.8 broadcast_in_dim.18
  5.0 0.1 multiply_convert_fusion
  5.1 0.8 scatter_custom_fusion
  5.9 0.1 reshape.78
  6.1 0.2 broadcast_in_dim.20
  6.3 1.3 %tile.11 = bf16[2,16,2,6144]{3,2,1,0:T(2,128)(2,1)} broadcast(bf16[16,2,6144]{2,1,0:T(2,128)(2,1)S(1)} %bitcast.12), dimensions={1,2,3} | broadcast | bytes 1179648 | tf_op jit(solution)/shard_map/tile | solution.py:110
  7.6 7.3 %all-to-all-start = ((bf16[32,2,6144]{2,1,0:T(2,128)(2,1)}), bf16[32,2,6144]{2,1,0:T(2,128)(2,1)S(1)}, u32[]{:S(2)}, u32[]{:S(2)}) async-start(bf16[32,2,6144]{2,1,0:T(2,128)(2,1)} %bitcast.4), calls=%async_computation | async-start | bytes 1572864 | tf_op jit(solution)/shard_map/all_to_all | solution.py:112
  14.9 21.5 %all-to-all-done = bf16[32,2,6144]{2,1,0:T(2,128)(2,1)S(1)} async-done(((bf16[32,2,6144]{2,1,0:T(2,128)(2,1)}), bf16[32,2,6144]{2,1,0:T(2,128)(2,1)S(1)}, u32[]{:S(2)}, u32[]{:S(2)}) %all-to-all-start) | async-done | bytes 786464 | tf_op jit(solution)/shard_map/all_to_all | solution.py:112
  36.4 0.3 reshape.79.x_ref.c_ref
  36.7 28.9 %shard_map.86 = bf16[64,6144]{1,0:T(8,128)(2,1)S(1)} custom-call(s32[1]{0:T(128)} %bitcast.offset_ref, bf16[64,6144]{1,0:T(8,128)(2,1)S(1)} %reshape.79.x_ref.c_ref, bf16[64,6144]{1,0:T(8,128)(2,1)S(1)} %reshape.79.x_ref.c_ref, bf16[4096,3072]{1,0:T(8,128)(2,1)} %wg_ref.1, bf16[4096,3072]{1,0:T(8,128)(2,1)} %wu_ref.1, bf16[4096,3072]{1,0:T(8,128)(2,1)} %wd_ref.1), custom_call_target="tpu_custom_call" | custom-call | flops 4831838208 | bytes 39321600 | tf_op jit(solution)/shard_map/pallas_call | solution.py:80
  65.6 1.4 %reshape.80 = bf16[32,2,6144]{2,1,0:T(2,128)(2,1)} reshape(bf16[64,6144]{1,0:T(8,128)(2,1)S(1)} %shard_map.86) | data formatting | bytes 1572864 | tf_op jit(solution)/shard_map/reshape | solution.py:114
  67.0 2.6 %all-to-all-start.1 = ((bf16[32,2,6144]{2,1,0:T(2,128)(2,1)}), bf16[32,2,6144]{2,1,0:T(2,128)(2,1)S(1)}, u32[]{:S(2)}, u32[]{:S(2)}) async-start(bf16[32,2,6144]{2,1,0:T(2,128)(2,1)} %reshape.80), calls=%async_computation.1 | async-start | bytes 1572864 | tf_op jit(solution)/shard_map/all_to_all | solution.py:115
  69.6 21.5 %all-to-all-done.1 = bf16[32,2,6144]{2,1,0:T(2,128)(2,1)S(1)} async-done(((bf16[32,2,6144]{2,1,0:T(2,128)(2,1)}), bf16[32,2,6144]{2,1,0:T(2,128)(2,1)S(1)}, u32[]{:S(2)}, u32[]{:S(2)}) %all-to-all-start.1) | async-done | bytes 786464 | tf_op jit(solution)/shard_map/all_to_all | solution.py:115
  91.1 0.7 convert_reduce_fusion
  91.8 0.3 reshape.81
  92.1 0.6 gather_fusion
  92.8 0.1 reshape.82
  92.9 0.9 slice_reduce_fusion
  (3 shorter events, 0.0 us)
Async XLA Ops:
  7.6 28.8 %all-to-all-start = ((bf16[32,2,6144]{2,1,0:T(2,128)(2,1)}), bf16[32,2,6144]{2,1,0:T(2,128)(2,1)S(1)}, u32[]{:S(2)}, u32[]{:S(2)}) async-start(bf16[32,2,6144]{2,1,0:T(2,128)(2,1)} %bitcast.4), calls=%async_computation | async-start | bytes 1572864 | tf_op jit(solution)/shard_map/all_to_all | solution.py:112
  67.0 24.1 %all-to-all-start.1 = ((bf16[32,2,6144]{2,1,0:T(2,128)(2,1)}), bf16[32,2,6144]{2,1,0:T(2,128)(2,1)S(1)}, u32[]{:S(2)}, u32[]{:S(2)}) async-start(bf16[32,2,6144]{2,1,0:T(2,128)(2,1)} %reshape.80), calls=%async_computation.1 | async-start | bytes 1572864 | tf_op jit(solution)/shard_map/all_to_all | solution.py:115

commit v3 on v2

--- a/solution.py
+++ b/solution.py
@@ -59,7 +59,7 @@
     m = rows.shape[0]
     hidden_units, features = w_gate.shape
     share = hidden_units // parts
-    block = min(256, share)
+    block = min(512, share)
     steps = share // block
     offset = jnp.reshape(part * steps, (1,)).astype(jnp.int32)
     row_spec = lambda half: pl.BlockSpec((m, features), lambda i, off: (0, half))
@@ -90,8 +90,6 @@
 
 def shards(tokens, cotangent, expert_ids, gate_weights, w_gate, w_up, w_down):
     devices = lax.axis_size("expert")
-    parts = lax.axis_size("groups")
-    part = lax.axis_index("groups")
     owner_count = devices // EXPERTS
     tok_count = tokens.shape[0]
     features = tokens.shape[1]
@@ -99,32 +97,25 @@
     routes = expert_ids.reshape(pair_count)
     rank_index = slot_ranks(routes)
     slot_index = routes * CAP + rank_index
-    token_pairs = jnp.repeat(tokens, 2, axis=0)
-    scaled = (
-        gate_weights.reshape(pair_count, 1).astype(jnp.float32)
-        * jnp.repeat(cotangent, 2, axis=0).astype(jnp.float32)
-    ).astype(jnp.bfloat16)
-    both = jnp.concatenate([token_pairs, scaled], axis=1)
-    slots = jnp.zeros((EXPERTS * CAP, 2 * features), jnp.bfloat16).at[slot_index].set(both)
-    send = jnp.repeat(slots.reshape(EXPERTS, CAP, 2 * features), owner_count, axis=0)
-    send = jnp.tile(send, (parts, 1, 1))
-    axes = ("groups", "expert")
-    recv = lax.all_to_all(send, axes, split_axis=0, concat_axis=0, tiled=True)
-    partials = expert_work(recv.reshape(-1, 2 * features), w_gate, w_up, w_down, part, parts)
-    back = partials.reshape(parts * devices, CAP, 2 * features)
-    home = lax.all_to_all(back, axes, split_axis=0, concat_axis=0, tiled=True)
-    sums = jnp.sum(
-        home.reshape(parts, EXPERTS, owner_count, CAP, 2 * features).astype(jnp.float32),
-        axis=(0, 2),
-    ).reshape(EXPERTS * CAP, 2 * features)
-    picked = sums[slot_index].reshape(tok_count, 2, 2 * features)
-    picked_out = picked[:, :, :features]
-    picked_grad = picked[:, :, features:]
-    layer_out = jnp.sum(picked_out * gate_weights.astype(jnp.float32)[:, :, None], axis=1).astype(
-        jnp.bfloat16
-    )
-    input_grad = jnp.sum(picked_grad, axis=1).astype(jnp.bfloat16)
-    return (layer_out, input_grad)
+    row_slot = (jnp.arange(devices * CAP) // (CAP * owner_count)) * CAP + jnp.arange(devices * CAP) % CAP
+    hit = (row_slot[:, None] == slot_index[None, :]).reshape(devices * CAP, tok_count, 2)
+    pick_tok = jnp.sum(hit, axis=2).astype(jnp.bfloat16)
+    pick_cot = jnp.sum(jnp.where(hit, gate_weights[None, :, :], 0), axis=2).astype(jnp.bfloat16)
+    send_tok = jnp.dot(pick_tok, tokens, preferred_element_type=jnp.float32)
+    send_cot = jnp.dot(pick_cot, cotangent, preferred_element_type=jnp.float32)
+    send = jnp.concatenate([send_tok, send_cot], axis=1).astype(jnp.bfloat16)
+    send = send.reshape(devices, CAP, 2 * features)
+    recv = lax.all_to_all(send, "expert", split_axis=0, concat_axis=0, tiled=True)
+    partials = expert_work(recv.reshape(-1, 2 * features), w_gate, w_up, w_down, 0, 1)
+    back = partials.reshape(devices, CAP, 2 * features)
+    home = lax.all_to_all(back, "expert", split_axis=0, concat_axis=0, tiled=True)
+    home = home.reshape(devices * CAP, 2 * features)
+    take = jnp.transpose(hit, (1, 2, 0))
+    take_out = jnp.sum(jnp.where(take, gate_weights[:, :, None], 0), axis=1).astype(jnp.bfloat16)
+    take_grad = jnp.sum(take, axis=1).astype(jnp.bfloat16)
+    layer_out = jnp.dot(take_out, home[:, :features], preferred_element_type=jnp.float32)
+    input_grad = jnp.dot(take_grad, home[:, features:], preferred_element_type=jnp.float32)
+    return (layer_out.astype(jnp.bfloat16), input_grad.astype(jnp.bfloat16))
 
 
 def solution(mesh):

time: 94.2 us -> 84 us (0.89)
  waiting for transfers between devices: 43 us -> 12 us
  blocking collectives: 0 us -> 19.4 us
  Pallas kernels: 28.9 us -> 41.2 us
  starting transfers between devices: 9.95 us -> 3.55 us
  local copies, waits for them, and re-layouts: 7.81 us -> 2.96 us
  matrix products: 0 us -> 2.67 us
  other arithmetic: 3.38 us -> 1.21 us
    all_to_all x2 -> x1, waiting for transfers between devices: 43 us -> 12 us  [shards(): lax.all_to_all(back, 'expert', split_axis=0, concat_axis=0, tiled=True)]
    all_to_all x0 -> x1, blocking collectives: none -> 19.4 us  [shards(): lax.all_to_all(send, 'expert', split_axis=0, concat_axis=0, tiled=True)]
    pallas_call x1, Pallas kernels: 28.9 us -> 41.2 us  [expert_work(): pl.pallas_call(expert_kernel, grid_spec=grid_spec, out_shape=jax.ShapeDty...]
    all_to_all x2 -> x1, starting transfers between devices: 9.95 us -> 3.55 us  [shards(): lax.all_to_all(back, 'expert', split_axis=0, concat_axis=0, tiled=True)]
    dot_general x0 -> x4, matrix products: none -> 2.67 us  [the longest x1 0.91 us: shards(): send_cot = jnp.dot(pick_cot, cotangent, preferred_element_type=jnp.float32)]
    broadcast_in_dim x3 -> x0, local copies, waits for them, and re-layouts: 1.74 us -> none  [the longest x1 0.77 us: shards(): token_pairs = jnp.repeat(tokens, 2, axis=0)]
    another operation x1 -> x0, local copies, waits for them, and re-layouts: 1.29 us -> none  [shards(): send = jnp.tile(send, (parts, 1, 1))]
    reshape x5 -> x2, local copies, waits for them, and re-layouts: 1.94 us -> 1.15 us  [the longest x1 1 us: shards(): back = partials.reshape(devices, CAP, 2 * features)]
  transfers between devices with their start and end apart: 2 -> 1, of which waited for: 2 -> 1; matrix products, arithmetic and copies ran while one was open for 0% -> 0% of each run, Pallas kernels for 0% -> 0%
where the time goes in v3:
time: 84 us; the launch traced here: 83.6 us
  Pallas kernels  41.2 us (49%)
  blocking collectives  19.4 us (23%)
  waiting for transfers between devices  12 us (14%)
  starting transfers between devices  3.55 us (4%)
  local copies, waits for them, and re-layouts  2.96 us (4%)
  matrix products  2.67 us (3%)
  other arithmetic  1.21 us (1%)
    pallas_call x1, Pallas kernels, expert_work(): pl.pallas_call(expert_kernel, grid_spec=grid_spec, out_shape=jax.ShapeDty...  41.2 us
    all_to_all x1, blocking collectives, shards(): lax.all_to_all(send, 'expert', split_axis=0, concat_axis=0, tiled=True)  19.4 us
    all_to_all x1, waiting for transfers between devices, shards(): lax.all_to_all(back, 'expert', split_axis=0, concat_axis=0, tiled=True)  12 us
    all_to_all x1, starting transfers between devices, shards(): lax.all_to_all(back, 'expert', split_axis=0, concat_axis=0, tiled=True)  3.55 us
  transfers between devices with their start and end apart: 1, of which 1 were waited for; matrix products, arithmetic and copies ran while one was open for 0% of the time, Pallas kernels for 0%

profile of v3, /device:TPU:0, one launch (start us, length us, event | category | flops | bytes accessed | tf_op | source)
XLA Modules:
  0.0 83.6 jit_solution(1426052321993396442)
XLA Ops:
  0.6 0.0 copy-start
  0.7 0.8 copy.30
  1.4 0.1 eq.39
  1.5 0.2 convert_reduce_fusion
  1.7 0.1 reduce_sum.54
  1.8 0.1 copy.32
  1.9 0.1 fusion.5
  2.0 0.0 copy-done
  2.0 0.3 convolution_convert_fusion.1
  2.2 0.1 concatenate.7
  2.4 0.7 fusion.8
  3.1 0.1 copy.34
  3.2 0.9 %convolution_convert_fusion = bf16[16,2,3072]{2,0,1:T(8,128)(2,1)S(1)} fusion(bf16[4,3072]{1,0:T(4,128)(2,1)} %param.8, bf16[16,2,4]{2,1,0:T(2,128)(2,1)S(1)} %bitcast.6), kind=kOutput, calls=%fused_computation | convolution fusion | flops 884736 | bytes 221440 | tf_op jit(solution)/shard_map/dot_general | solution.py:105
  4.2 0.4 copy.37
  4.6 19.4 %all_to_all.10 = bf16[16,2,6144]{2,1,0:T(2,128)(2,1)S(1)} all-to-all(bf16[16,2,6144]{2,1,0:T(2,128)(2,1)S(1)} %copy.37), channel_id=1, replica_groups=mesh['groups'=2,'expert'=16] {'expert'}, dimensions={0} | all-to-all | bytes 786432 | tf_op jit(solution)/shard_map/all_to_all | solution.py:108
  23.9 0.1 reshape.66.x_ref.c_ref
  24.1 0.0 copy-start.1
  24.1 41.2 %shard_map.86 = bf16[32,6144]{1,0:T(8,128)(2,1)S(1)} custom-call(s32[1]{0:T(128)} %constant.40.clone.1.offset_ref, bf16[32,6144]{1,0:T(8,128)(2,1)S(1)} %reshape.66.x_ref.c_ref, bf16[32,6144]{1,0:T(8,128)(2,1)S(1)} %reshape.66.x_ref.c_ref, bf16[4096,3072]{1,0:T(8,128)(2,1)} %wg_ref.1, bf16[4096,3072]{1,0:T(8,128)(2,1)} %wu_ref.1, bf16[4096,3072]{1,0:T(8,128)(2,1)} %wd_ref.1), custom_call_target="tpu_custom_call" | custom-call | flops 4831838208 | bytes 76283904 | tf_op jit(solution)/shard_map/pallas_call | solution.py:80
  65.3 1.0 %reshape.67 = bf16[16,2,6144]{2,1,0:T(2,128)(2,1)} reshape(bf16[32,6144]{1,0:T(8,128)(2,1)S(1)} %shard_map.86) | data formatting | bytes 786432 | tf_op jit(solution)/shard_map/reshape | solution.py:110
  66.3 3.6 %all-to-all-start.1 = ((bf16[16,2,6144]{2,1,0:T(2,128)(2,1)}), bf16[16,2,6144]{2,1,0:T(2,128)(2,1)S(1)}, u32[]{:S(2)}, u32[]{:S(2)}) async-start(bf16[16,2,6144]{2,1,0:T(2,128)(2,1)} %reshape.67), calls=%async_computation.1 | async-start | bytes 786432 | tf_op jit(solution)/shard_map/all_to_all | solution.py:111
  69.8 0.1 fusion.4
  69.9 0.0 copy-done.1
  69.9 0.1 fusion.7
  70.0 12.0 %all-to-all-done.1 = bf16[16,2,6144]{2,1,0:T(2,128)(2,1)S(1)} async-done(((bf16[16,2,6144]{2,1,0:T(2,128)(2,1)}), bf16[16,2,6144]{2,1,0:T(2,128)(2,1)S(1)}, u32[]{:S(2)}, u32[]{:S(2)}) %all-to-all-start.1) | async-done | bytes 393248 | tf_op jit(solution)/shard_map/all_to_all | solution.py:111
  82.0 0.1 reshape.68
  82.1 0.8 convolution_convert_fusion.2
  82.9 0.8 convolution_convert_fusion.3
  (4 shorter events, 0.1 us)
Async XLA Ops:
  0.6 1.3 %copy-start = (bf16[4,3072]{1,0:T(4,128)(2,1)S(1)}, bf16[4,3072]{1,0:T(4,128)(2,1)}, u32[]{:S(2)}) copy-start(bf16[4,3072]{1,0:T(4,128)(2,1)} %param.7) | copy-start | bytes 73732
  24.1 45.9 %copy-start.1 = (bf16[4,2]{0,1:T(2,128)(2,1)S(1)}, bf16[4,2]{0,1:T(2,128)(2,1)}, u32[]{:S(2)}) copy-start(bf16[4,2]{0,1:T(2,128)(2,1)} %param.10) | copy-start | bytes 52
  66.3 15.7 %all-to-all-start.1 = ((bf16[16,2,6144]{2,1,0:T(2,128)(2,1)}), bf16[16,2,6144]{2,1,0:T(2,128)(2,1)S(1)}, u32[]{:S(2)}, u32[]{:S(2)}) async-start(bf16[16,2,6144]{2,1,0:T(2,128)(2,1)} %reshape.67), calls=%async_computation.1 | async-start | bytes 786432 | tf_op jit(solution)/shard_map/all_to_all | solution.py:111

commit v4 on v3

--- a/solution.py
+++ b/solution.py
@@ -29,8 +29,9 @@
         acc_out[...] = jnp.zeros_like(acc_out)
         acc_grad[...] = jnp.zeros_like(acc_grad)
 
-    x = x_ref[...]
-    c = c_ref[...]
+    m = acc_out.shape[0]
+    x = x_ref[...].reshape(m, features)
+    c = c_ref[...].reshape(m, features)
     wg = wg_ref[...]
     wu = wu_ref[...]
     wd = wd_ref[...]
@@ -51,20 +52,22 @@
 
     @pl.when(step == pl.num_programs(0) - 1)
     def _():
-        out_ref[:, :features] = acc_out[...].astype(out_ref.dtype)
-        out_ref[:, features:] = acc_grad[...].astype(out_ref.dtype)
+        rows = out_ref.shape[:2]
+        out_ref[:, :, :features] = acc_out[...].astype(out_ref.dtype).reshape(rows + (features,))
+        out_ref[:, :, features:] = acc_grad[...].astype(out_ref.dtype).reshape(rows + (features,))
 
 
 def expert_work(rows, w_gate, w_up, w_down, part, parts):
-    m = rows.shape[0]
+    chunks, cap = rows.shape[:2]
+    m = chunks * cap
     hidden_units, features = w_gate.shape
     share = hidden_units // parts
     block = min(512, share)
     steps = share // block
     offset = jnp.reshape(part * steps, (1,)).astype(jnp.int32)
-    row_spec = lambda half: pl.BlockSpec((m, features), lambda i, off: (0, half))
+    row_spec = lambda half: pl.BlockSpec((chunks, cap, features), lambda i, off: (0, 0, half))
     w_spec = pl.BlockSpec((block, features), lambda i, off: (off[0] + i, 0))
-    out_spec = pl.BlockSpec((m, 2 * features), lambda i, off: (0, 0))
+    out_spec = pl.BlockSpec((chunks, cap, 2 * features), lambda i, off: (0, 0, 0))
     cost = pl.CostEstimate(
         flops=12 * m * share * features,
         transcendentals=m * share,
@@ -80,7 +83,7 @@
     return pl.pallas_call(
         expert_kernel,
         grid_spec=grid_spec,
-        out_shape=jax.ShapeDtypeStruct((m, 2 * features), jnp.bfloat16),
+        out_shape=jax.ShapeDtypeStruct((chunks, cap, 2 * features), jnp.bfloat16),
         compiler_params=pltpu.CompilerParams(
             dimension_semantics=("arbitrary",), vmem_limit_bytes=48 * 1024 * 1024
         ),
@@ -88,34 +91,86 @@
     )(offset, rows, rows, w_gate, w_up, w_down)
 
 
+def pack_kernel(owner_count, ids_ref, gw_ref, tok_ref, cot_ref, out_ref):
+    features = tok_ref.shape[1]
+    pairs = ids_ref.shape[0]
+    out_ref[...] = jnp.zeros_like(out_ref)
+    for p in range(pairs):
+        e = ids_ref[p]
+        rank = jnp.int32(0)
+        for q in range(p):
+            rank = rank + (ids_ref[q] == e).astype(jnp.int32)
+        t = p // 2
+        tok_row = tok_ref[t:t + 1, :]
+        cot_row = (gw_ref[p] * cot_ref[t:t + 1, :].astype(jnp.float32)).astype(out_ref.dtype)
+        for j in range(owner_count):
+            o = e * owner_count + j
+            for r in range(CAP):
+                keep = rank == r
+                out_ref[o, r:r + 1, :features] = jnp.where(keep, tok_row, out_ref[o, r:r + 1, :features])
+                out_ref[o, r:r + 1, features:] = jnp.where(keep, cot_row, out_ref[o, r:r + 1, features:])
+
+def unpack_kernel(owner_count, ids_ref, gw_ref, home_ref, out_ref, grad_ref):
+    features = out_ref.shape[1]
+    pairs = ids_ref.shape[0]
+    for t in range(pairs // 2):
+        total_out = jnp.zeros((1, features), jnp.float32)
+        total_grad = jnp.zeros((1, features), jnp.float32)
+        for k in range(2):
+            p = 2 * t + k
+            e = ids_ref[p]
+            rank = jnp.int32(0)
+            for q in range(p):
+                rank = rank + (ids_ref[q] == e).astype(jnp.int32)
+            part_out = jnp.zeros((1, features), jnp.float32)
+            part_grad = jnp.zeros((1, features), jnp.float32)
+            for j in range(owner_count):
+                block = home_ref[e * owner_count + j].astype(jnp.float32)
+                row = jnp.where(rank == 0, block[0:1], block[1:2])
+                part_out = part_out + row[:, :features]
+                part_grad = part_grad + row[:, features:]
+            total_out = total_out + gw_ref[p] * part_out
+            total_grad = total_grad + part_grad
+        out_ref[t:t + 1, :] = total_out.astype(out_ref.dtype)
+        grad_ref[t:t + 1, :] = total_grad.astype(grad_ref.dtype)
+
+SMEM_SPEC = pl.BlockSpec(memory_space=pltpu.SMEM)
+VMEM_SPEC = pl.BlockSpec(memory_space=pltpu.VMEM)
+
+def pack(tokens, cotangent, expert_ids, gate_weights, devices):
+    owner_count = devices // EXPERTS
+    tok_count, features = tokens.shape
+    ids = expert_ids.reshape(-1).astype(jnp.int32)
+    gw = gate_weights.reshape(-1).astype(jnp.float32)
+    return pl.pallas_call(
+        functools.partial(pack_kernel, owner_count),
+        in_specs=[SMEM_SPEC, SMEM_SPEC, VMEM_SPEC, VMEM_SPEC],
+        out_specs=VMEM_SPEC,
+        out_shape=jax.ShapeDtypeStruct((devices, CAP, 2 * features), tokens.dtype),
+    )(ids, gw, tokens, cotangent)
+
+def unpack(home, expert_ids, gate_weights, devices):
+    owner_count = devices // EXPERTS
+    tok_count = expert_ids.shape[0]
+    features = home.shape[2] // 2
+    ids = expert_ids.reshape(-1).astype(jnp.int32)
+    gw = gate_weights.reshape(-1).astype(jnp.float32)
+    return pl.pallas_call(
+        functools.partial(unpack_kernel, owner_count),
+        in_specs=[SMEM_SPEC, SMEM_SPEC, VMEM_SPEC],
+        out_specs=[VMEM_SPEC, VMEM_SPEC],
+        out_shape=[jax.ShapeDtypeStruct((tok_count, features), home.dtype)] * 2,
+    )(ids, gw, home)
+
+
 def shards(tokens, cotangent, expert_ids, gate_weights, w_gate, w_up, w_down):
     devices = lax.axis_size("expert")
-    owner_count = devices // EXPERTS
-    tok_count = tokens.shape[0]
-    features = tokens.shape[1]
-    pair_count = tok_count * 2
-    routes = expert_ids.reshape(pair_count)
-    rank_index = slot_ranks(routes)
-    slot_index = routes * CAP + rank_index
-    row_slot = (jnp.arange(devices * CAP) // (CAP * owner_count)) * CAP + jnp.arange(devices * CAP) % CAP
-    hit = (row_slot[:, None] == slot_index[None, :]).reshape(devices * CAP, tok_count, 2)
-    pick_tok = jnp.sum(hit, axis=2).astype(jnp.bfloat16)
-    pick_cot = jnp.sum(jnp.where(hit, gate_weights[None, :, :], 0), axis=2).astype(jnp.bfloat16)
-    send_tok = jnp.dot(pick_tok, tokens, preferred_element_type=jnp.float32)
-    send_cot = jnp.dot(pick_cot, cotangent, preferred_element_type=jnp.float32)
-    send = jnp.concatenate([send_tok, send_cot], axis=1).astype(jnp.bfloat16)
-    send = send.reshape(devices, CAP, 2 * features)
+    send = pack(tokens, cotangent, expert_ids, gate_weights, devices)
     recv = lax.all_to_all(send, "expert", split_axis=0, concat_axis=0, tiled=True)
-    partials = expert_work(recv.reshape(-1, 2 * features), w_gate, w_up, w_down, 0, 1)
-    back = partials.reshape(devices, CAP, 2 * features)
-    home = lax.all_to_all(back, "expert", split_axis=0, concat_axis=0, tiled=True)
-    home = home.reshape(devices * CAP, 2 * features)
-    take = jnp.transpose(hit, (1, 2, 0))
-    take_out = jnp.sum(jnp.where(take, gate_weights[:, :, None], 0), axis=1).astype(jnp.bfloat16)
-    take_grad = jnp.sum(take, axis=1).astype(jnp.bfloat16)
-    layer_out = jnp.dot(take_out, home[:, :features], preferred_element_type=jnp.float32)
-    input_grad = jnp.dot(take_grad, home[:, features:], preferred_element_type=jnp.float32)
-    return (layer_out.astype(jnp.bfloat16), input_grad.astype(jnp.bfloat16))
+    partials = expert_work(recv, w_gate, w_up, w_down, 0, 1)
+    home = lax.all_to_all(partials, "expert", split_axis=0, concat_axis=0, tiled=True)
+    layer_out, input_grad = unpack(home, expert_ids, gate_weights, devices)
+    return (layer_out, input_grad)
 
 
 def solution(mesh):

time: 84 us -> 84.1 us (level)
  blocking collectives: 19.4 us -> 35 us
  waiting for transfers between devices: 12 us -> 0 us
  Pallas kernels: 41.2 us -> 45.3 us
  starting transfers between devices: 3.55 us -> 0 us
  matrix products: 2.67 us -> 0 us
  other arithmetic: 1.21 us -> 0 us
    all_to_all x0 -> x1, blocking collectives: none -> 15.5 us  [shards(): lax.all_to_all(partials, 'expert', split_axis=0, concat_axis=0, tiled=True)]
    all_to_all x1 -> x0, waiting for transfers between devices: 12 us -> none  [shards(): lax.all_to_all(back, 'expert', split_axis=0, concat_axis=0, tiled=True)]
    pallas_call x0 -> x2, Pallas kernels: none -> 4 us  [the longest x1 2.21 us: pack(): pl.pallas_call(functools.partial(pack_kernel, owner_count), in_specs=[SME...]
    all_to_all x1 -> x0, starting transfers between devices: 3.55 us -> none  [shards(): lax.all_to_all(back, 'expert', split_axis=0, concat_axis=0, tiled=True)]
    dot_general x4 -> x0, matrix products: 2.67 us -> none  [the longest x1 0.91 us: shards(): send_cot = jnp.dot(pick_cot, cotangent, preferred_element_type=jnp.float32)]
    convert_element_type x0 -> x2, local copies, waits for them, and re-layouts: none -> 1.35 us  [unpack(): gw = gate_weights.reshape(-1).astype(jnp.float32)]
    reduce_sum x5 -> x0, other arithmetic: 1.17 us -> none  [the longest x1 0.74 us: shards(): jnp.sum(jnp.where(hit, gate_weights[None, :, :], 0), axis=2)]
  transfers between devices with their start and end apart: 1 -> 0, of which waited for: 1 -> 0; matrix products, arithmetic and copies ran while one was open for 0% -> 0% of each run, Pallas kernels for 0% -> 0%
where the time goes in v4:
time: 84.1 us; the launch traced here: 83.7 us
  Pallas kernels  45.3 us (54%)
  blocking collectives  35 us (42%)
  local copies, waits for them, and re-layouts  2.78 us (3%)
    pallas_call x1, Pallas kernels, expert_work(): pl.pallas_call(expert_kernel, grid_spec=grid_spec, out_shape=jax.ShapeDty...  41.3 us
    all_to_all x1, blocking collectives, shards(): lax.all_to_all(send, 'expert', split_axis=0, concat_axis=0, tiled=True)  19.5 us
    all_to_all x1, blocking collectives, shards(): lax.all_to_all(partials, 'expert', split_axis=0, concat_axis=0, tiled=True)  15.5 us
    pallas_call x1, Pallas kernels, pack(): pl.pallas_call(functools.partial(pack_kernel, owner_count), in_specs=[SME...  2.21 us
    pallas_call x1, Pallas kernels, unpack(): pl.pallas_call(functools.partial(unpack_kernel, owner_count), in_specs=[S...  1.79 us

profile of v4, /device:TPU:0, one launch (start us, length us, event | category | flops | bytes accessed | tf_op | source)
XLA Modules:
  0.0 83.7 jit_solution(15542763888755641364)
XLA Ops:
  0.6 0.8 copy.11
  1.4 0.7 reshape.12.ids_ref
  2.1 0.7 copy.12
  2.8 0.6 reshape.13.gw_ref
  3.4 2.2 %shard_map.86 = bf16[16,2,6144]{2,1,0:T(2,128)(2,1)} custom-call(s32[8]{0:T(128)} %reshape.12.ids_ref, f32[8]{0:T(128)} %reshape.13.gw_ref, bf16[4,3072]{1,0:T(4,128)(2,1)} %tok_ref.1, bf16[4,3072]{1,0:T(4,128)(2,1)} %cot_ref.1), custom_call_target="tpu_custom_call" | custom-call | tf_op jit(solution)/shard_map/pallas_call | solution.py:145
  5.6 19.5 %all_to_all.10.x_ref.c_ref = bf16[16,2,6144]{2,1,0:T(2,128)(2,1)S(1)} all-to-all(bf16[16,2,6144]{2,1,0:T(2,128)(2,1)} %shard_map.86), channel_id=1, replica_groups=mesh['groups'=2,'expert'=16] {'expert'}, dimensions={0} | all-to-all | bytes 786432 | tf_op jit(solution)/shard_map/all_to_all | solution.py:169
  25.2 41.3 %shard_map.87 = bf16[16,2,6144]{2,1,0:T(2,128)(2,1)S(1)} custom-call(s32[1]{0:T(128)} %constant.0.clone.1.offset_ref, bf16[16,2,6144]{2,1,0:T(2,128)(2,1)S(1)} %all_to_all.10.x_ref.c_ref, bf16[16,2,6144]{2,1,0:T(2,128)(2,1)S(1)} %all_to_all.10.x_ref.c_ref, bf16[4096,3072]{1,0:T(8,128)(2,1)} %wg_ref.1, bf16[4096,3072]{1,0:T(8,128)(2,1)} %wu_ref.1, ...), custom_call_target="tpu_custom_call" | custom-call | flops 4831838208 | bytes 76283904 | tf_op jit(solution)/shard_map/pallas_call | solution.py:83
  66.5 15.5 %all_to_all.11.home_ref = bf16[16,2,6144]{2,1,0:T(2,128)(2,1)} all-to-all(bf16[16,2,6144]{2,1,0:T(2,128)(2,1)S(1)} %shard_map.87), channel_id=1, replica_groups=mesh['groups'=2,'expert'=16] {'expert'}, dimensions={0} | all-to-all | bytes 786432 | tf_op jit(solution)/shard_map/all_to_all | solution.py:171
  81.9 1.8 %shard_map.88 = (bf16[4,3072]{1,0:T(4,128)(2,1)}, bf16[4,3072]{1,0:T(4,128)(2,1)}) custom-call(s32[8]{0:T(128)} %reshape.12.ids_ref, f32[8]{0:T(128)} %reshape.13.gw_ref, bf16[16,2,6144]{2,1,0:T(2,128)(2,1)} %all_to_all.11.home_ref), custom_call_target="tpu_custom_call" | custom-call | tf_op jit(solution)/shard_map/pallas_call | solution.py:158

commit v5 on v4

--- a/solution.py
+++ b/solution.py
@@ -91,18 +91,23 @@
     )(offset, rows, rows, w_gate, w_up, w_down)
 
 
+def pair_rank(ids_ref, p):
+    e = ids_ref[p % 2, p // 2]
+    rank = jnp.int32(0)
+    for q in range(p):
+        rank = rank + (ids_ref[q % 2, q // 2] == e).astype(jnp.int32)
+    return e, rank
+
+
 def pack_kernel(owner_count, ids_ref, gw_ref, tok_ref, cot_ref, out_ref):
-    features = tok_ref.shape[1]
-    pairs = ids_ref.shape[0]
+    tok_count, features = tok_ref.shape
     out_ref[...] = jnp.zeros_like(out_ref)
-    for p in range(pairs):
-        e = ids_ref[p]
-        rank = jnp.int32(0)
-        for q in range(p):
-            rank = rank + (ids_ref[q] == e).astype(jnp.int32)
-        t = p // 2
+    gw = gw_ref[...].astype(jnp.float32)
+    for p in range(2 * tok_count):
+        e, rank = pair_rank(ids_ref, p)
+        t, k = p // 2, p % 2
         tok_row = tok_ref[t:t + 1, :]
-        cot_row = (gw_ref[p] * cot_ref[t:t + 1, :].astype(jnp.float32)).astype(out_ref.dtype)
+        cot_row = (gw[k:k + 1, t:t + 1] * cot_ref[t:t + 1, :].astype(jnp.float32)).astype(out_ref.dtype)
         for j in range(owner_count):
             o = e * owner_count + j
             for r in range(CAP):
@@ -110,18 +115,15 @@
                 out_ref[o, r:r + 1, :features] = jnp.where(keep, tok_row, out_ref[o, r:r + 1, :features])
                 out_ref[o, r:r + 1, features:] = jnp.where(keep, cot_row, out_ref[o, r:r + 1, features:])
 
+
 def unpack_kernel(owner_count, ids_ref, gw_ref, home_ref, out_ref, grad_ref):
-    features = out_ref.shape[1]
-    pairs = ids_ref.shape[0]
-    for t in range(pairs // 2):
+    tok_count, features = out_ref.shape
+    gw = gw_ref[...].astype(jnp.float32)
+    for t in range(tok_count):
         total_out = jnp.zeros((1, features), jnp.float32)
         total_grad = jnp.zeros((1, features), jnp.float32)
         for k in range(2):
-            p = 2 * t + k
-            e = ids_ref[p]
-            rank = jnp.int32(0)
-            for q in range(p):
-                rank = rank + (ids_ref[q] == e).astype(jnp.int32)
+            e, rank = pair_rank(ids_ref, 2 * t + k)
             part_out = jnp.zeros((1, features), jnp.float32)
             part_grad = jnp.zeros((1, features), jnp.float32)
             for j in range(owner_count):
@@ -129,38 +131,37 @@
                 row = jnp.where(rank == 0, block[0:1], block[1:2])
                 part_out = part_out + row[:, :features]
                 part_grad = part_grad + row[:, features:]
-            total_out = total_out + gw_ref[p] * part_out
+            total_out = total_out + gw[k:k + 1, t:t + 1] * part_out
             total_grad = total_grad + part_grad
         out_ref[t:t + 1, :] = total_out.astype(out_ref.dtype)
         grad_ref[t:t + 1, :] = total_grad.astype(grad_ref.dtype)
 
+
 SMEM_SPEC = pl.BlockSpec(memory_space=pltpu.SMEM)
 VMEM_SPEC = pl.BlockSpec(memory_space=pltpu.VMEM)
 
+
 def pack(tokens, cotangent, expert_ids, gate_weights, devices):
     owner_count = devices // EXPERTS
-    tok_count, features = tokens.shape
-    ids = expert_ids.reshape(-1).astype(jnp.int32)
-    gw = gate_weights.reshape(-1).astype(jnp.float32)
+    features = tokens.shape[1]
     return pl.pallas_call(
         functools.partial(pack_kernel, owner_count),
-        in_specs=[SMEM_SPEC, SMEM_SPEC, VMEM_SPEC, VMEM_SPEC],
+        in_specs=[SMEM_SPEC, VMEM_SPEC, VMEM_SPEC, VMEM_SPEC],
         out_specs=VMEM_SPEC,
         out_shape=jax.ShapeDtypeStruct((devices, CAP, 2 * features), tokens.dtype),
-    )(ids, gw, tokens, cotangent)
+    )(expert_ids.T, gate_weights.T, tokens, cotangent)
+
 
 def unpack(home, expert_ids, gate_weights, devices):
     owner_count = devices // EXPERTS
     tok_count = expert_ids.shape[0]
     features = home.shape[2] // 2
-    ids = expert_ids.reshape(-1).astype(jnp.int32)
-    gw = gate_weights.reshape(-1).astype(jnp.float32)
     return pl.pallas_call(
         functools.partial(unpack_kernel, owner_count),
-        in_specs=[SMEM_SPEC, SMEM_SPEC, VMEM_SPEC],
+        in_specs=[SMEM_SPEC, VMEM_SPEC, VMEM_SPEC],
         out_specs=[VMEM_SPEC, VMEM_SPEC],
         out_shape=[jax.ShapeDtypeStruct((tok_count, features), home.dtype)] * 2,
-    )(ids, gw, home)
+    )(expert_ids.T, gate_weights.T, home)
 
 
 def shards(tokens, cotangent, expert_ids, gate_weights, w_gate, w_up, w_down):

time: 84.1 us -> 81.4 us (0.968)
  local copies, waits for them, and re-layouts: 2.78 us -> 0 us
    convert_element_type x2 -> x0, local copies, waits for them, and re-layouts: 1.35 us -> none  [unpack(): gw = gate_weights.reshape(-1).astype(jnp.float32)]
where the time goes in v5:
time: 81.4 us; the launch traced here: 81.1 us
  Pallas kernels  45.4 us (56%)
  blocking collectives  35 us (43%)
    pallas_call x1, Pallas kernels, expert_work(): pl.pallas_call(expert_kernel, grid_spec=grid_spec, out_shape=jax.ShapeDty...  41.3 us
    all_to_all x1, blocking collectives, shards(): lax.all_to_all(send, 'expert', split_axis=0, concat_axis=0, tiled=True)  19.5 us
    all_to_all x1, blocking collectives, shards(): lax.all_to_all(partials, 'expert', split_axis=0, concat_axis=0, tiled=True)  15.5 us
    pallas_call x1, Pallas kernels, pack(): pl.pallas_call(functools.partial(pack_kernel, owner_count), in_specs=[SME...  2.3 us
    pallas_call x1, Pallas kernels, unpack(): pl.pallas_call(functools.partial(unpack_kernel, owner_count), in_specs=[S...  1.82 us

profile of v5, /device:TPU:0, one launch (start us, length us, event | category | flops | bytes accessed | tf_op | source)
XLA Modules:
  0.0 81.1 jit_solution(5063525863037842414)
XLA Ops:
  0.6 2.3 %shard_map.86 = bf16[16,2,6144]{2,1,0:T(2,128)(2,1)} custom-call(s32[2,4]{1,0:T(2,128)} %bitcast.2, bf16[2,4]{1,0:T(2,128)(2,1)} %bitcast.4, bf16[4,3072]{1,0:T(4,128)(2,1)} %tok_ref.1, bf16[4,3072]{1,0:T(4,128)(2,1)} %cot_ref.1), custom_call_target="tpu_custom_call" | custom-call | tf_op jit(solution)/shard_map/pallas_call | solution.py:147
  2.9 19.5 %all_to_all.10.x_ref.c_ref = bf16[16,2,6144]{2,1,0:T(2,128)(2,1)S(1)} all-to-all(bf16[16,2,6144]{2,1,0:T(2,128)(2,1)} %shard_map.86), channel_id=1, replica_groups=mesh['groups'=2,'expert'=16] {'expert'}, dimensions={0} | all-to-all | bytes 786432 | tf_op jit(solution)/shard_map/all_to_all | solution.py:170
  22.5 41.3 %shard_map.87 = bf16[16,2,6144]{2,1,0:T(2,128)(2,1)S(1)} custom-call(s32[1]{0:T(128)} %constant.0.clone.1.offset_ref, bf16[16,2,6144]{2,1,0:T(2,128)(2,1)S(1)} %all_to_all.10.x_ref.c_ref, bf16[16,2,6144]{2,1,0:T(2,128)(2,1)S(1)} %all_to_all.10.x_ref.c_ref, bf16[4096,3072]{1,0:T(8,128)(2,1)} %wg_ref.1, bf16[4096,3072]{1,0:T(8,128)(2,1)} %wu_ref.1, ...), custom_call_target="tpu_custom_call" | custom-call | flops 4831838208 | bytes 76283904 | tf_op jit(solution)/shard_map/pallas_call | solution.py:83
  63.8 15.5 %all_to_all.11.home_ref = bf16[16,2,6144]{2,1,0:T(2,128)(2,1)} all-to-all(bf16[16,2,6144]{2,1,0:T(2,128)(2,1)S(1)} %shard_map.87), channel_id=1, replica_groups=mesh['groups'=2,'expert'=16] {'expert'}, dimensions={0} | all-to-all | bytes 786432 | tf_op jit(solution)/shard_map/all_to_all | solution.py:172
  79.3 1.8 %shard_map.88 = (bf16[4,3072]{1,0:T(4,128)(2,1)}, bf16[4,3072]{1,0:T(4,128)(2,1)}) custom-call(s32[2,4]{1,0:T(2,128)} %bitcast.3, bf16[2,4]{1,0:T(2,128)(2,1)} %bitcast.5, bf16[16,2,6144]{2,1,0:T(2,128)(2,1)} %all_to_all.11.home_ref), custom_call_target="tpu_custom_call" | custom-call | tf_op jit(solution)/shard_map/pallas_call | solution.py:159
